TPU v7x, 32 devices: a whole 2x2x4 slice. The times are simulated.
32 devices in a mesh: groups: 2 (over y), sec: 4 (over z), strip: 2 (over x), chan: 2 (over core).
Axes of the slice: x: 2, y: 2, z: 4, core: 2. Of those that a mesh axis runs over, the one named last changes fastest.
Arguments:
- sections: bfloat16 [16, 16, 1024], P(('groups', 'sec'), 'strip'), parts along dimension 0, may hold values from -64 to 64
- w_first: bfloat16 [32, 9], replicated, may hold values from -2 to 2
- w_second: bfloat16 [9, 32, 32], replicated, may hold values from -0.375 to 0.375
- offsets: int32 [16, 2, 16, 1024], P(('groups', 'sec'), None, 'strip'), parts along dimension 0, may hold values from -32 to 31
Outputs:
- warped: bfloat16 [16, 32, 16, 1024], P(('groups', 'sec'), 'chan', 'strip'), parts along dimension 0
- composed: float32 [16, 2, 16, 1024], P(('groups', 'sec'), None, 'strip'), parts along dimension 0
There are 2 independent parts, one for each index of `groups`. A program takes and returns all parts, laid end to end along the dimension named above; an argument that names none is the same for every part. Nothing has to cross between parts.
All inputs are finite; a program needn't handle non-finite values.
Results may differ from a plain program's by a relative error of at most 0.0083.
Values may be sent and summed in bfloat16 or wider, within the bound.
No kernel may reach another device: no remote copies, remote signals or barrier semaphores. Data moves between devices by JAX's collectives and lax.ppermute only.
A program may use at most 64 MiB of HBM per device.

v0:
```python
import jax
import jax.numpy as jnp
from jax import lax
from jax.sharding import PartitionSpec as P

score_scale = 4.0


def with_halo(cells, sides, width):
    for axis, dim in sides:
        count = lax.axis_size(axis)
        ends = count - 1
        head = lax.slice_in_dim(cells, 0, width, axis=dim)
        tail = lax.slice_in_dim(cells, cells.shape[dim] - width, cells.shape[dim], axis=dim)
        cells = jnp.concatenate(
            [
                lax.ppermute(tail, axis, [(i, (i + 1) % count) for i in range(ends)]),
                cells,
                lax.ppermute(head, axis, [((i + 1) % count, i) for i in range(ends)]),
            ],
            axis=dim,
        )
    return cells


def from_behind(value, axis, by):
    length = lax.axis_size(axis)
    pairs = [(i, i + by) for i in range(length) if 0 <= i + by < length]
    return lax.ppermute(value, axis, pairs)


def first_taps(extended, rows_out, row_start):
    columns = extended.shape[-1]
    padded = jnp.pad(extended, ((0, 0), (0, 0), (2, 2)))
    tap_list = []
    for shift_y in (-2, 0, 2):
        for shift_x in (-2, 0, 2):
            tap_list.append(
                padded[
                    :,
                    row_start + shift_y : row_start + shift_y + rows_out,
                    2 + shift_x : 2 + shift_x + columns,
                ]
            )
    return jnp.stack(tap_list)


def second_terms(weights, inputs):
    rows_out = inputs.shape[2] - 2
    columns = inputs.shape[3]
    padded = jnp.pad(inputs, ((0, 0), (0, 0), (0, 0), (1, 1)))
    summed = None
    tap_index = 0
    for shift_y in (-1, 0, 1):
        for shift_x in (-1, 0, 1):
            window = padded[
                :, :, 1 + shift_y : 1 + shift_y + rows_out, 1 + shift_x : 1 + shift_x + columns
            ]
            tap_term = jnp.einsum(
                "oi,ispw->ospw", weights[tap_index], window, preferred_element_type=jnp.float32
            )
            summed = tap_term if summed is None else summed + tap_term
            tap_index += 1
    return summed


def hat_weights(quant_row):
    base = jnp.floor_divide(quant_row, 8)
    frac = (quant_row - 8 * base).astype(jnp.float32) * 0.125
    return [
        jnp.where(base == shift, 1.0 - frac, 0.0) + jnp.where(base + 1 == shift, frac, 0.0)
        for shift in range(-4, 5)
    ]


def sample(source, quant, row_start):
    rows_out, columns = (quant.shape[1], quant.shape[2])
    hats_y = hat_weights(quant[0])
    hats_x = hat_weights(quant[1])
    summed = jnp.zeros((source.shape[0], rows_out, columns), jnp.float32)
    for index_x in range(9):
        inner = jnp.zeros((source.shape[0], rows_out, columns), jnp.float32)
        for index_y in range(9):
            lower = row_start + index_y - 4
            window = source[:, lower : lower + rows_out, index_x : index_x + columns].astype(
                jnp.float32
            )
            inner = inner + hats_y[index_y] * window
        summed = summed + hats_x[index_x] * inner
    return summed


def local(sections, w_first, w_second, offsets):
    sec_local, strip_rows, columns = sections.shape
    chan_count = lax.axis_size("chan")
    own_index = lax.axis_index("chan")
    head_width = w_second.shape[1] // chan_count
    strip_first = lax.axis_index("strip") * strip_rows
    total_rows = strip_rows * lax.axis_size("strip")
    extended = with_halo(sections, (("strip", 1),), 3)
    tap_stack = first_taps(extended, strip_rows + 2, 2)
    global_rows = strip_first - 1 + lax.broadcasted_iota(jnp.int32, (strip_rows + 2, 1), 0)
    inside = (global_rows >= 0) & (global_rows < total_rows)
    all_maps = jnp.einsum("ct,tspw->cspw", w_first, tap_stack, preferred_element_type=jnp.float32)
    all_maps = jnp.where(inside, jnp.maximum(all_maps, 0.0), 0.0).astype(jnp.bfloat16)
    w_outputs = lax.dynamic_slice_in_dim(w_second, own_index * head_width, head_width, 1)
    mixed_sum = second_terms(w_outputs, all_maps)
    own_features = jnp.maximum(mixed_sum, 0.0).astype(jnp.bfloat16)
    previous_features = from_behind(own_features[:, sec_local - 1 :], "sec", 1)
    features = jnp.concatenate([previous_features, own_features], axis=1)
    framed = with_halo(features, (("strip", 2),), 4)
    current = framed[:, 1:, 4 : 4 + strip_rows, :]
    earlier = jnp.pad(framed[:, :sec_local], ((0, 0), (0, 0), (0, 0), (4, 4)))
    factor = score_scale / head_width
    field_shape = (sec_local, strip_rows, columns)
    running_max = jnp.full(field_shape, -1e30, jnp.float32)
    weight_sum = jnp.zeros(field_shape, jnp.float32)
    along_y = jnp.zeros(field_shape, jnp.float32)
    along_x = jnp.zeros(field_shape, jnp.float32)
    step_cols = lax.broadcasted_iota(jnp.float32, (9, 1, 1, 1), 0) - 4.0
    for shift_y in range(9):
        scores = (
            jnp.stack(
                [
                    jnp.einsum(
                        "cspw,cspw->spw",
                        current,
                        earlier[:, :, shift_y : shift_y + strip_rows, shift_x : shift_x + columns],
                        preferred_element_type=jnp.float32,
                    )
                    for shift_x in range(9)
                ]
            )
            * factor
        )
        highest = jnp.maximum(running_max, jnp.max(scores, axis=0))
        rescale = jnp.exp(running_max - highest)
        weights = jnp.exp(scores - highest)
        block_sum = jnp.sum(weights, axis=0)
        weight_sum = weight_sum * rescale + block_sum
        along_y = along_y * rescale + (shift_y - 4.0) * block_sum
        along_x = along_x * rescale + jnp.sum(weights * step_cols, axis=0)
        running_max = highest
    head_flow = jnp.stack([along_y / weight_sum, along_x / weight_sum], axis=1)
    flow_field = lax.psum(head_flow.astype(jnp.bfloat16), "chan").astype(jnp.float32) / chan_count
    warped_list = []
    for local_sec in range(sec_local):
        source = jnp.pad(framed[:, local_sec + 1], ((0, 0), (0, 0), (4, 4)))
        warped_list.append(sample(source, offsets[local_sec], 4).astype(jnp.bfloat16))
    warped = jnp.stack(warped_list)
    reach_all = 4 * sec_local
    reach_src = 4 * (sec_local - 1)
    rim_stack = with_halo(
        jnp.concatenate([flow_field, offsets.astype(jnp.float32)], axis=1).astype(jnp.bfloat16),
        (("strip", 2),),
        reach_src,
    ).astype(jnp.float32)
    row_ids = (
        strip_first
        - reach_src
        + lax.broadcasted_iota(jnp.int32, (strip_rows + 2 * reach_src, 1), 0)
    )

    def compose(incoming):
        source = with_halo(incoming.astype(jnp.bfloat16), (("strip", 1),), reach_all).astype(
            incoming.dtype
        )
        results = []
        for local_sec in range(sec_local):
            reach = 4 * (sec_local - 1 - local_sec)
            lower = reach_src - reach
            span = strip_rows + 2 * reach
            portion = rim_stack[local_sec, :, lower : lower + span]
            quant = portion[2:].astype(jnp.int32)
            updated = (
                portion[:2]
                + portion[2:] * 0.125
                + sample(jnp.pad(source, ((0, 0), (0, 0), (4, 4))), quant, 4)
            )
            global_rows = row_ids[lower : lower + span]
            valid_rows = (global_rows >= 0) & (global_rows < total_rows)
            updated = jnp.where(valid_rows, updated, 0.0)
            source = updated
            results.append(updated[:, reach : reach + strip_rows])
        return jnp.stack(results)

    def chain_turn(turn, state_pair):
        incoming = from_behind(state_pair[0].astype(jnp.bfloat16), "sec", 1).astype(jnp.float32)
        composed_all = compose(incoming)
        return (composed_all[sec_local - 1], composed_all)

    start_pair = (
        jnp.zeros((2, strip_rows, columns), jnp.float32),
        jnp.zeros((sec_local, 2, strip_rows, columns), jnp.float32),
    )
    composed = lax.fori_loop(0, lax.axis_size("sec"), chain_turn, start_pair)[1]
    return (warped, composed)


def solution(mesh):
    in_specs = (
        P(("groups", "sec"), "strip", None),
        P(),
        P(),
        P(("groups", "sec"), None, "strip", None),
    )
    out_specs = (
        P(("groups", "sec"), "chan", "strip", None),
        P(("groups", "sec"), None, "strip", None),
    )
    return jax.shard_map(local, mesh=mesh, in_specs=in_specs, out_specs=out_specs, check_vma=False)
```

profile of v0, /device:TPU:10, one launch (start us, length us, event | category | flops | bytes accessed | tf_op | source)
XLA Modules:
  0.0 182.5 jit_solution(9279792757851363367)
XLA Ops:
  8.1 2.4 %collective-permute-start.4 = (bf16[2,3,1024]{2,1,0:T(4,128)(2,1)S(1)}, bf16[2,3,1024]{2,1,0:T(4,128)(2,1)S(1)}, u32[]{:S(2)}, u32[]{:S(2)}) collective-permute-start(bf16[2,3,1024]{2,1,0:T(4,128)(2,1)S(1)} %get-tuple-element.606), channel_id=1, source_target_pairs={{2,0},{3,1},{6,4},{7,5},{10,8},{11,9},{14,12},{15,13},{18,16},{19,... | collective-permute-start | bytes 36872 | tf_op jit(solution)/shard_map/ppermute | solution.py:19
  12.0 4.2 %collective-permute-done.3 = bf16[2,3,1024]{2,1,0:T(4,128)(2,1)S(1)} collective-permute-done((bf16[2,3,1024]{2,1,0:T(4,128)(2,1)S(1)}, bf16[2,3,1024]{2,1,0:T(4,128)(2,1)S(1)}, u32[]{:S(2)}, u32[]{:S(2)}) %collective-permute-start.3) | collective-permute-done | bytes 12320 | tf_op jit(solution)/shard_map/ppermute | solution.py:17
  25.1 3.5 %collective-permute-start.5 = (bf16[16,1,8,1024]{3,0,2,1:T(8,128)(2,1)S(1)}, bf16[16,1,8,1024]{3,0,2,1:T(8,128)(2,1)S(1)}, u32[]{:S(2)}, u32[]{:S(2)}) collective-permute-start(bf16[16,1,8,1024]{3,0,2,1:T(8,128)(2,1)S(1)} %slice.2649), channel_id=1, source_target_pairs={{0,4},{4,8},{8,12},{1,5},{5,9},{9,13},{2,6},{6,10},{10,14},{3,7},{... | collective-permute-start | bytes 786440 | tf_op jit(solution)/shard_map/ppermute | solution.py:29
  29.5 4.1 %collective-permute-done.5 = bf16[16,1,8,1024]{3,0,2,1:T(8,128)(2,1)S(1)} collective-permute-done((bf16[16,1,8,1024]{3,0,2,1:T(8,128)(2,1)S(1)}, bf16[16,1,8,1024]{3,0,2,1:T(8,128)(2,1)S(1)}, u32[]{:S(2)}, u32[]{:S(2)}) %collective-permute-start.5) | collective-permute-done | bytes 262176 | tf_op jit(solution)/shard_map/ppermute | solution.py:29
  37.2 4.7 %collective-permute-done.7 = bf16[16,3,4,1024]{3,0,2,1:T(8,128)(2,1)S(1)} collective-permute-done((bf16[16,3,4,1024]{3,0,2,1:T(8,128)(2,1)S(1)}, bf16[16,3,4,1024]{3,0,2,1:T(8,128)(2,1)S(1)}, u32[]{:S(2)}, u32[]{:S(2)}) %collective-permute-start.7) | collective-permute-done | bytes 393248 | tf_op jit(solution)/shard_map/ppermute | solution.py:19
  41.9 4.1 %collective-permute-done.6 = bf16[16,3,4,1024]{3,0,2,1:T(8,128)(2,1)S(1)} collective-permute-done((bf16[16,3,4,1024]{3,0,2,1:T(8,128)(2,1)S(1)}, bf16[16,3,4,1024]{3,0,2,1:T(8,128)(2,1)S(1)}, u32[]{:S(2)}, u32[]{:S(2)}) %collective-permute-start.6) | collective-permute-done | bytes 393248 | tf_op jit(solution)/shard_map/ppermute | solution.py:17
  46.4 3.0 %fusion.345 = (f32[2,8,1024]{2,1,0:T(8,128)S(1)}, f32[2,8,1024]{2,1,0:T(8,128)S(1)}, f32[2,8,1024]{2,1,0:T(8,128)S(1)}, f32[2,8,1024]{2,1,0:T(8,128)S(1)}, f32[2...) fusion(bf16[16,2,8,1024]{3,0,2,1:T(8,128)(2,1)S(1)} %fusion.336, ...), kind=kLoop, calls=%fused_computation.661 | loop fusion | flops 7192576 | bytes 2162688 | tf_op jit(solution)/shard_map/cspw,cspw->spw/dot_general | solution.py:125
  49.4 2.8 %fusion.408 = (f32[2,8,1024]{2,1,0:T(8,128)S(1)}, f32[2,8,1024]{2,1,0:T(8,128)S(1)}, f32[2,8,1024]{2,1,0:T(8,128)S(1)}, f32[2,8,1024]{2,1,0:T(8,128)S(1)}, f32[2...) fusion(bf16[16,2,8,1024]{3,0,2,1:T(8,128)(2,1)S(1)} %fusion.336, ...), kind=kLoop, calls=%fused_computation.724 | loop fusion | flops 7192576 | bytes 2162688 | tf_op jit(solution)/shard_map/cspw,cspw->spw/dot_general | solution.py:125
  52.2 2.7 %fusion.397 = (f32[2,8,1024]{2,1,0:T(8,128)S(1)}, f32[2,8,1024]{2,1,0:T(8,128)S(1)}, f32[2,8,1024]{2,1,0:T(8,128)S(1)}, f32[2,8,1024]{2,1,0:T(8,128)S(1)}, f32[2...) fusion(bf16[16,2,8,1024]{3,0,2,1:T(8,128)(2,1)S(1)} %fusion.336, ...), kind=kLoop, calls=%fused_computation.713 | loop fusion | flops 7192576 | bytes 2162688 | tf_op jit(solution)/shard_map/cspw,cspw->spw/dot_general | solution.py:125
  54.9 2.7 %fusion.407 = (f32[2,8,1024]{2,1,0:T(8,128)S(1)}, f32[2,8,1024]{2,1,0:T(8,128)S(1)}, f32[2,8,1024]{2,1,0:T(8,128)S(1)}, f32[2,8,1024]{2,1,0:T(8,128)S(1)}, f32[2...) fusion(bf16[16,2,8,1024]{3,0,2,1:T(8,128)(2,1)S(1)} %fusion.336, ...), kind=kLoop, calls=%fused_computation.723 | loop fusion | flops 7192576 | bytes 2162688 | tf_op jit(solution)/shard_map/cspw,cspw->spw/dot_general | solution.py:125
  57.6 2.8 %fusion.376 = (f32[2,8,1024]{2,1,0:T(8,128)S(1)}, f32[2,8,1024]{2,1,0:T(8,128)S(1)}, f32[2,8,1024]{2,1,0:T(8,128)S(1)}, f32[2,8,1024]{2,1,0:T(8,128)S(1)}, f32[2...) fusion(bf16[16,2,8,1024]{3,0,2,1:T(8,128)(2,1)S(1)} %fusion.336, ...), kind=kLoop, calls=%fused_computation.692 | loop fusion | flops 7192576 | bytes 2162688 | tf_op jit(solution)/shard_map/cspw,cspw->spw/dot_general | solution.py:125
  60.5 2.8 %fusion.387 = (f32[2,8,1024]{2,1,0:T(8,128)S(1)}, f32[2,8,1024]{2,1,0:T(8,128)S(1)}, f32[2,8,1024]{2,1,0:T(8,128)S(1)}, f32[2,8,1024]{2,1,0:T(8,128)S(1)}, f32[2...) fusion(bf16[16,2,8,1024]{3,0,2,1:T(8,128)(2,1)S(1)} %fusion.336, ...), kind=kLoop, calls=%fused_computation.703 | loop fusion | flops 7192576 | bytes 2162688 | tf_op jit(solution)/shard_map/cspw,cspw->spw/dot_general | solution.py:125
  63.3 2.8 %fusion.356 = (f32[2,8,1024]{2,1,0:T(8,128)S(1)}, f32[2,8,1024]{2,1,0:T(8,128)S(1)}, f32[2,8,1024]{2,1,0:T(8,128)S(1)}, f32[2,8,1024]{2,1,0:T(8,128)S(1)}, f32[2...) fusion(bf16[16,2,8,1024]{3,0,2,1:T(8,128)(2,1)S(1)} %fusion.336, ...), kind=kLoop, calls=%fused_computation.672 | loop fusion | flops 7192576 | bytes 2162688 | tf_op jit(solution)/shard_map/cspw,cspw->spw/dot_general | solution.py:125
  66.0 2.9 %fusion.366 = (f32[2,8,1024]{2,1,0:T(8,128)S(1)}, f32[2,8,1024]{2,1,0:T(8,128)S(1)}, f32[2,8,1024]{2,1,0:T(8,128)S(1)}, f32[2,8,1024]{2,1,0:T(8,128)S(1)}, f32[2...) fusion(bf16[16,2,8,1024]{3,0,2,1:T(8,128)(2,1)S(1)} %fusion.336, ...), kind=kLoop, calls=%fused_computation.682 | loop fusion | flops 7192576 | bytes 2162688 | tf_op jit(solution)/shard_map/cspw,cspw->spw/dot_general | solution.py:125
  75.5 7.0 %fusion.447 = bf16[1,16,8,1024]{3,1,2,0:T(8,128)(2,1)S(1)} fusion(f32[8,1024]{1,0:T(8,128)S(1)} %copy-done.10, f32[8,1024]{1,0:T(8,128)S(1)} %get-tuple-element.567, f32[8,1024]{1,0:T(8,128)S(1)} %get-tuple-element.566, f32[8,1024]{1,0:T(8,128)S(1)} %get-tuple-element.565, bf16[16,16,1024]{2,0,1:T(8,128)(2,1)S(1)} %get-tuple-element.540, ...), kind=kLoop, calls=%fused_computation.825 | loop fusion | flops 33030144 | bytes 3735552 | tf_op jit(solution)/shard_map/stack | solution.py:150
  82.6 7.0 %fusion.446 = bf16[1,16,8,1024]{3,1,2,0:T(8,128)(2,1)S(1)} fusion(f32[8,1024]{1,0:T(8,128)S(1)} %copy-done.8, f32[8,1024]{1,0:T(8,128)S(1)} %copy-done.7, f32[8,1024]{1,0:T(8,128)S(1)} %copy-done.6, f32[8,1024]{1,0:T(8,128)S(1)} %copy-done.5, bf16[16,16,1024]{2,0,1:T(8,128)(2,1)S(1)} %get-tuple-element.539, f32[8,1024]{1,0:T(8,128)S(1)} %copy-done.4, ...), kind=kLoop, calls=%fused_computation.824 | loop fusion | flops 33030144 | bytes 3735552 | tf_op jit(solution)/shard_map/stack | solution.py:150
  89.6 5.0 %all-reduce.9.cloned.1.call-done = bf16[2,2,8,1024]{3,2,0,1:T(8,128)(2,1)} async-done(((bf16[2,2,8,1024]{3,2,0,1:T(8,128)(2,1)}), bf16[2,2,8,1024]{3,2,0,1:T(8,128)(2,1)}) %all-reduce.9.cloned.1.call-update) | async-done | bytes 65552 | tf_op jit(solution)/shard_map/psum | solution.py:145
  95.5 2.5 %collective-permute-start.9 = (bf16[2,4,4,1024]{3,2,0,1:T(4,128)(2,1)S(1)}, bf16[2,4,4,1024]{3,2,0,1:T(4,128)(2,1)S(1)}, u32[]{:S(2)}, u32[]{:S(2)}) collective-permute-start(bf16[2,4,4,1024]{3,2,0,1:T(4,128)(2,1)S(1)} %get-tuple-element.554), channel_id=1, source_target_pairs={{2,0},{3,1},{6,4},{7,5},{10,8},{11,9},{14,12},{15,13},{18,16},{19,... | collective-permute-start | bytes 196616 | tf_op jit(solution)/shard_map/ppermute | solution.py:19
  100.4 3.7 %collective-permute-done.8 = bf16[2,4,4,1024]{3,2,0,1:T(4,128)(2,1)S(1)} collective-permute-done((bf16[2,4,4,1024]{3,2,0,1:T(4,128)(2,1)S(1)}, bf16[2,4,4,1024]{3,2,0,1:T(4,128)(2,1)S(1)}, u32[]{:S(2)}, u32[]{:S(2)}) %collective-permute-start.8) | collective-permute-done | bytes 65568 | tf_op jit(solution)/shard_map/ppermute | solution.py:17
  104.4 71.3 %while.16 = (s32[]{:T(128)}, f32[2,8,1024]{2,1,0:T(8,128)S(1)}, f32[2,2,8,1024]{3,2,1,0:T(8,128)}, s32[16,1]{0,1:T(1,128)S(1)}, f32[2,4,16,1024]{3,2,1,0:T(8,128...) while((s32[]{:T(128)}, f32[2,8,1024]{2,1,0:T(8,128)S(1)}, ...), condition=%wide.region_29.30_spmd.clone, body=%wide.region_28.29_spmd.clone.sunk | while | flops 12337227 | bytes 8586647 | solution.py:196
  104.7 3.4 %collective-permute-start = (bf16[2,8,1024]{2,1,0:T(8,128)(2,1)S(1)}, bf16[2,8,1024]{2,1,0:T(8,128)(2,1)S(1)}, u32[]{:S(2)}, u32[]{:S(2)}) collective-permute-start(bf16[2,8,1024]{2,1,0:T(8,128)(2,1)S(1)} %select_convert_fusion.3), channel_id=1, source_target_pairs={{0,4},{4,8},{8,12},{1,5},{5,9},{9,13},{2,6},{6,10},{10,14},{3,7},{... | collective-permute-start | bytes 98312 | tf_op jit(solution)/shard_map/while/body/eval_jaxpr/ppermute | solution.py:29
  113.6 4.2 %collective-permute-done.2 = bf16[2,8,1024]{2,1,0:T(8,128)(2,1)S(1)} collective-permute-done((bf16[2,8,1024]{2,1,0:T(8,128)(2,1)S(1)}, bf16[2,8,1024]{2,1,0:T(8,128)(2,1)S(1)}, u32[]{:S(2)}, u32[]{:S(2)}) %collective-permute-start.2) | collective-permute-done | bytes 32800 | tf_op jit(solution)/shard_map/while/body/eval_jaxpr/ppermute | solution.py:17
  117.9 2.5 %fusion.537 = f32[2,16,1024]{2,1,0:T(8,128)S(1)} fusion(f32[2,24,1024]{2,1,0:T(8,128)S(1)} %maximum_convert_fusion.3, f32[2,4,16,1024]{3,2,1,0:T(8,128)S(1)} %get-tuple-element.838, f32[16,1024]{1,0:T(8,128)S(1)} %get-tuple-element.762, f32[16,1024]{1,0:T(8,128)S(1)} %get-tuple-element.763, f32[16,1024]{1,0:T(8,128)S(1)} %get-tuple-element.764, ...), kind=kLoop, calls=%fused_computation.244.clone.1 | loop fusion | flops 5701632 | bytes 2949632 | tf_op jit(solution)/shard_map/while/body/eval_jaxpr/jit(_where)/select_n | solution.py:182
  122.4 3.4 %collective-permute-start = (bf16[2,8,1024]{2,1,0:T(8,128)(2,1)S(1)}, bf16[2,8,1024]{2,1,0:T(8,128)(2,1)S(1)}, u32[]{:S(2)}, u32[]{:S(2)}) collective-permute-start(bf16[2,8,1024]{2,1,0:T(8,128)(2,1)S(1)} %select_convert_fusion.3), channel_id=1, source_target_pairs={{0,4},{4,8},{8,12},{1,5},{5,9},{9,13},{2,6},{6,10},{10,14},{3,7},{... | collective-permute-start | bytes 98312 | tf_op jit(solution)/shard_map/while/body/eval_jaxpr/ppermute | solution.py:29
  131.4 4.2 %collective-permute-done.2 = bf16[2,8,1024]{2,1,0:T(8,128)(2,1)S(1)} collective-permute-done((bf16[2,8,1024]{2,1,0:T(8,128)(2,1)S(1)}, bf16[2,8,1024]{2,1,0:T(8,128)(2,1)S(1)}, u32[]{:S(2)}, u32[]{:S(2)}) %collective-permute-start.2) | collective-permute-done | bytes 32800 | tf_op jit(solution)/shard_map/while/body/eval_jaxpr/ppermute | solution.py:17
  135.6 2.5 %fusion.537 = f32[2,16,1024]{2,1,0:T(8,128)S(1)} fusion(f32[2,24,1024]{2,1,0:T(8,128)S(1)} %maximum_convert_fusion.3, f32[2,4,16,1024]{3,2,1,0:T(8,128)S(1)} %get-tuple-element.838, f32[16,1024]{1,0:T(8,128)S(1)} %get-tuple-element.762, f32[16,1024]{1,0:T(8,128)S(1)} %get-tuple-element.763, f32[16,1024]{1,0:T(8,128)S(1)} %get-tuple-element.764, ...), kind=kLoop, calls=%fused_computation.244.clone.1 | loop fusion | flops 5701632 | bytes 2949632 | tf_op jit(solution)/shard_map/while/body/eval_jaxpr/jit(_where)/select_n | solution.py:182
  140.2 3.4 %collective-permute-start = (bf16[2,8,1024]{2,1,0:T(8,128)(2,1)S(1)}, bf16[2,8,1024]{2,1,0:T(8,128)(2,1)S(1)}, u32[]{:S(2)}, u32[]{:S(2)}) collective-permute-start(bf16[2,8,1024]{2,1,0:T(8,128)(2,1)S(1)} %select_convert_fusion.3), channel_id=1, source_target_pairs={{0,4},{4,8},{8,12},{1,5},{5,9},{9,13},{2,6},{6,10},{10,14},{3,7},{... | collective-permute-start | bytes 98312 | tf_op jit(solution)/shard_map/while/body/eval_jaxpr/ppermute | solution.py:29
  149.1 4.2 %collective-permute-done.2 = bf16[2,8,1024]{2,1,0:T(8,128)(2,1)S(1)} collective-permute-done((bf16[2,8,1024]{2,1,0:T(8,128)(2,1)S(1)}, bf16[2,8,1024]{2,1,0:T(8,128)(2,1)S(1)}, u32[]{:S(2)}, u32[]{:S(2)}) %collective-permute-start.2) | collective-permute-done | bytes 32800 | tf_op jit(solution)/shard_map/while/body/eval_jaxpr/ppermute | solution.py:17
  153.4 2.5 %fusion.537 = f32[2,16,1024]{2,1,0:T(8,128)S(1)} fusion(f32[2,24,1024]{2,1,0:T(8,128)S(1)} %maximum_convert_fusion.3, f32[2,4,16,1024]{3,2,1,0:T(8,128)S(1)} %get-tuple-element.838, f32[16,1024]{1,0:T(8,128)S(1)} %get-tuple-element.762, f32[16,1024]{1,0:T(8,128)S(1)} %get-tuple-element.763, f32[16,1024]{1,0:T(8,128)S(1)} %get-tuple-element.764, ...), kind=kLoop, calls=%fused_computation.244.clone.1 | loop fusion | flops 5701632 | bytes 2949632 | tf_op jit(solution)/shard_map/while/body/eval_jaxpr/jit(_where)/select_n | solution.py:182
  157.9 3.4 %collective-permute-start = (bf16[2,8,1024]{2,1,0:T(8,128)(2,1)S(1)}, bf16[2,8,1024]{2,1,0:T(8,128)(2,1)S(1)}, u32[]{:S(2)}, u32[]{:S(2)}) collective-permute-start(bf16[2,8,1024]{2,1,0:T(8,128)(2,1)S(1)} %select_convert_fusion.3), channel_id=1, source_target_pairs={{0,4},{4,8},{8,12},{1,5},{5,9},{9,13},{2,6},{6,10},{10,14},{3,7},{... | collective-permute-start | bytes 98312 | tf_op jit(solution)/shard_map/while/body/eval_jaxpr/ppermute | solution.py:29
  166.9 4.2 %collective-permute-done.2 = bf16[2,8,1024]{2,1,0:T(8,128)(2,1)S(1)} collective-permute-done((bf16[2,8,1024]{2,1,0:T(8,128)(2,1)S(1)}, bf16[2,8,1024]{2,1,0:T(8,128)(2,1)S(1)}, u32[]{:S(2)}, u32[]{:S(2)}) %collective-permute-start.2) | collective-permute-done | bytes 32800 | tf_op jit(solution)/shard_map/while/body/eval_jaxpr/ppermute | solution.py:17
  171.1 2.5 %fusion.537 = f32[2,16,1024]{2,1,0:T(8,128)S(1)} fusion(f32[2,24,1024]{2,1,0:T(8,128)S(1)} %maximum_convert_fusion.3, f32[2,4,16,1024]{3,2,1,0:T(8,128)S(1)} %get-tuple-element.838, f32[16,1024]{1,0:T(8,128)S(1)} %get-tuple-element.762, f32[16,1024]{1,0:T(8,128)S(1)} %get-tuple-element.763, f32[16,1024]{1,0:T(8,128)S(1)} %get-tuple-element.764, ...), kind=kLoop, calls=%fused_computation.244.clone.1 | loop fusion | flops 5701632 | bytes 2949632 | tf_op jit(solution)/shard_map/while/body/eval_jaxpr/jit(_where)/select_n | solution.py:182
  (250 shorter events, 55.2 us)
Async XLA Ops:
  7.2 14.1 %copy-start = (bf16[9,32,32]{2,1,0:T(8,128)(2,1)S(1)}, bf16[9,32,32]{2,1,0:T(8,128)(2,1)}, u32[]{:S(2)}) copy-start(bf16[9,32,32]{2,1,0:T(8,128)(2,1)} %param.8) | copy-start | bytes 55300
  7.2 87.4 %all-reduce.9.cloned.1.call-start = ((), (), s32[]{:S(2)}) async-start(), calls=%async_computation | async-start | bytes 131072 | tf_op jit(solution)/shard_map/psum | solution.py:145
  8.1 3.9 %collective-permute-start.4 = (bf16[2,3,1024]{2,1,0:T(4,128)(2,1)S(1)}, bf16[2,3,1024]{2,1,0:T(4,128)(2,1)S(1)}, u32[]{:S(2)}, u32[]{:S(2)}) collective-permute-start(bf16[2,3,1024]{2,1,0:T(4,128)(2,1)S(1)} %get-tuple-element.606), channel_id=1, source_target_pairs={{2,0},{3,1},{6,4},{7,5},{10,8},{11,9},{14,12},{15,13},{18,16},{19,... | collective-permute-start | bytes 36872 | tf_op jit(solution)/shard_map/ppermute | solution.py:19
  10.5 5.6 %collective-permute-start.3 = (bf16[2,3,1024]{2,1,0:T(4,128)(2,1)S(1)}, bf16[2,3,1024]{2,1,0:T(4,128)(2,1)S(1)}, u32[]{:S(2)}, u32[]{:S(2)}) collective-permute-start(bf16[2,3,1024]{2,1,0:T(4,128)(2,1)S(1)} %get-tuple-element.605), channel_id=1, source_target_pairs={{0,2},{1,3},{4,6},{5,7},{8,10},{9,11},{12,14},{13,15},{16,18},{17,... | collective-permute-start | bytes 36872 | tf_op jit(solution)/shard_map/ppermute | solution.py:17
  18.2 2.5 %copy-start.16 = (bf16[32,9]{0,1:T(8,128)(2,1)S(1)}, bf16[32,9]{0,1:T(8,128)(2,1)}, u32[]{:S(2)}) copy-start(bf16[32,9]{0,1:T(8,128)(2,1)} %param.7) | copy-start | bytes 1732
  24.5 4.0 %copy-start.1 = (s32[2,2,8,1024]{3,2,1,0:T(8,128)S(1)}, s32[2,2,8,1024]{3,2,1,0:T(8,128)}, u32[]{:S(2)}) copy-start(s32[2,2,8,1024]{3,2,1,0:T(8,128)} %param.9) | copy-start | bytes 393220
  25.1 8.5 %collective-permute-start.5 = (bf16[16,1,8,1024]{3,0,2,1:T(8,128)(2,1)S(1)}, bf16[16,1,8,1024]{3,0,2,1:T(8,128)(2,1)S(1)}, u32[]{:S(2)}, u32[]{:S(2)}) collective-permute-start(bf16[16,1,8,1024]{3,0,2,1:T(8,128)(2,1)S(1)} %slice.2649), channel_id=1, source_target_pairs={{0,4},{4,8},{8,12},{1,5},{5,9},{9,13},{2,6},{6,10},{10,14},{3,7},{... | collective-permute-start | bytes 786440 | tf_op jit(solution)/shard_map/ppermute | solution.py:29
  33.6 8.2 %collective-permute-start.7 = (bf16[16,3,4,1024]{3,0,2,1:T(8,128)(2,1)S(1)}, bf16[16,3,4,1024]{3,0,2,1:T(8,128)(2,1)S(1)}, u32[]{:S(2)}, u32[]{:S(2)}) collective-permute-start(bf16[16,3,4,1024]{3,0,2,1:T(8,128)(2,1)S(1)} %get-tuple-element.544), channel_id=1, source_target_pairs={{2,0},{3,1},{6,4},{7,5},{10,8},{11,9},{14,12},{15,13},{18,16},{19,... | collective-permute-start | bytes 1179656 | tf_op jit(solution)/shard_map/ppermute | solution.py:19
  35.6 10.4 %collective-permute-start.6 = (bf16[16,3,4,1024]{3,0,2,1:T(8,128)(2,1)S(1)}, bf16[16,3,4,1024]{3,0,2,1:T(8,128)(2,1)S(1)}, u32[]{:S(2)}, u32[]{:S(2)}) collective-permute-start(bf16[16,3,4,1024]{3,0,2,1:T(8,128)(2,1)S(1)} %get-tuple-element.543), channel_id=1, source_target_pairs={{0,2},{1,3},{4,6},{5,7},{8,10},{9,11},{12,14},{13,15},{16,18},{17,... | collective-permute-start | bytes 1179656 | tf_op jit(solution)/shard_map/ppermute | solution.py:17
  74.4 0.9 copy-start.11
  75.4 7.1 %copy-start.2 = (f32[8,1024]{1,0:T(8,128)S(1)}, f32[8,1024]{1,0:T(8,128)}, u32[]{:S(2)}) copy-start(f32[8,1024]{1,0:T(8,128)} %get-tuple-element.577) | copy-start | bytes 98308
  75.4 7.1 %copy-start.3 = (f32[8,1024]{1,0:T(8,128)S(1)}, f32[8,1024]{1,0:T(8,128)}, u32[]{:S(2)}) copy-start(f32[8,1024]{1,0:T(8,128)} %get-tuple-element.578) | copy-start | bytes 98308
  75.4 7.1 %copy-start.4 = (f32[8,1024]{1,0:T(8,128)S(1)}, f32[8,1024]{1,0:T(8,128)}, u32[]{:S(2)}) copy-start(f32[8,1024]{1,0:T(8,128)} %get-tuple-element.579) | copy-start | bytes 98308
  75.4 7.1 %copy-start.5 = (f32[8,1024]{1,0:T(8,128)S(1)}, f32[8,1024]{1,0:T(8,128)}, u32[]{:S(2)}) copy-start(f32[8,1024]{1,0:T(8,128)} %get-tuple-element.580) | copy-start | bytes 98308
  75.4 7.1 %copy-start.6 = (f32[8,1024]{1,0:T(8,128)S(1)}, f32[8,1024]{1,0:T(8,128)}, u32[]{:S(2)}) copy-start(f32[8,1024]{1,0:T(8,128)} %get-tuple-element.581) | copy-start | bytes 98308
  75.4 7.1 %copy-start.7 = (f32[8,1024]{1,0:T(8,128)S(1)}, f32[8,1024]{1,0:T(8,128)}, u32[]{:S(2)}) copy-start(f32[8,1024]{1,0:T(8,128)} %get-tuple-element.582) | copy-start | bytes 98308
  75.5 7.1 %copy-start.8 = (f32[8,1024]{1,0:T(8,128)S(1)}, f32[8,1024]{1,0:T(8,128)}, u32[]{:S(2)}) copy-start(f32[8,1024]{1,0:T(8,128)} %get-tuple-element.583) | copy-start | bytes 98308
  75.5 7.1 %copy-start.9 = (f32[8,1024]{1,0:T(8,128)S(1)}, f32[8,1024]{1,0:T(8,128)}, u32[]{:S(2)}) copy-start(f32[8,1024]{1,0:T(8,128)} %get-tuple-element.584) | copy-start | bytes 98308
  95.5 4.9 %collective-permute-start.9 = (bf16[2,4,4,1024]{3,2,0,1:T(4,128)(2,1)S(1)}, bf16[2,4,4,1024]{3,2,0,1:T(4,128)(2,1)S(1)}, u32[]{:S(2)}, u32[]{:S(2)}) collective-permute-start(bf16[2,4,4,1024]{3,2,0,1:T(4,128)(2,1)S(1)} %get-tuple-element.554), channel_id=1, source_target_pairs={{2,0},{3,1},{6,4},{7,5},{10,8},{11,9},{14,12},{15,13},{18,16},{19,... | collective-permute-start | bytes 196616 | tf_op jit(solution)/shard_map/ppermute | solution.py:19
  98.0 6.2 %collective-permute-start.8 = (bf16[2,4,4,1024]{3,2,0,1:T(4,128)(2,1)S(1)}, bf16[2,4,4,1024]{3,2,0,1:T(4,128)(2,1)S(1)}, u32[]{:S(2)}, u32[]{:S(2)}) collective-permute-start(bf16[2,4,4,1024]{3,2,0,1:T(4,128)(2,1)S(1)} %get-tuple-element.553), channel_id=1, source_target_pairs={{0,2},{1,3},{4,6},{5,7},{8,10},{9,11},{12,14},{13,15},{16,18},{17,... | collective-permute-start | bytes 196616 | tf_op jit(solution)/shard_map/ppermute | solution.py:17
  104.7 5.8 %collective-permute-start = (bf16[2,8,1024]{2,1,0:T(8,128)(2,1)S(1)}, bf16[2,8,1024]{2,1,0:T(8,128)(2,1)S(1)}, u32[]{:S(2)}, u32[]{:S(2)}) collective-permute-start(bf16[2,8,1024]{2,1,0:T(8,128)(2,1)S(1)} %select_convert_fusion.3), channel_id=1, source_target_pairs={{0,4},{4,8},{8,12},{1,5},{5,9},{9,13},{2,6},{6,10},{10,14},{3,7},{... | collective-permute-start | bytes 98312 | tf_op jit(solution)/shard_map/while/body/eval_jaxpr/ppermute | solution.py:29
  110.5 3.1 %collective-permute-start.1 = (bf16[2,8,1024]{2,1,0:T(8,128)(2,1)S(1)}, bf16[2,8,1024]{2,1,0:T(8,128)(2,1)S(1)}, u32[]{:S(2)}, u32[]{:S(2)}) collective-permute-start(bf16[2,8,1024]{2,1,0:T(8,128)(2,1)S(1)} %collective-permute-done), channel_id=1, source_target_pairs={{2,0},{3,1},{6,4},{7,5},{10,8},{11,9},{14,12},{15,13},{18,16},{19,... | collective-permute-start | bytes 98312 | tf_op jit(solution)/shard_map/while/body/eval_jaxpr/ppermute | solution.py:19
  112.1 5.8 %collective-permute-start.2 = (bf16[2,8,1024]{2,1,0:T(8,128)(2,1)S(1)}, bf16[2,8,1024]{2,1,0:T(8,128)(2,1)S(1)}, u32[]{:S(2)}, u32[]{:S(2)}) collective-permute-start(bf16[2,8,1024]{2,1,0:T(8,128)(2,1)S(1)} %collective-permute-done), channel_id=1, source_target_pairs={{0,2},{1,3},{4,6},{5,7},{8,10},{9,11},{12,14},{13,15},{16,18},{17,... | collective-permute-start | bytes 98312 | tf_op jit(solution)/shard_map/while/body/eval_jaxpr/ppermute | solution.py:17
  122.4 5.8 %collective-permute-start = (bf16[2,8,1024]{2,1,0:T(8,128)(2,1)S(1)}, bf16[2,8,1024]{2,1,0:T(8,128)(2,1)S(1)}, u32[]{:S(2)}, u32[]{:S(2)}) collective-permute-start(bf16[2,8,1024]{2,1,0:T(8,128)(2,1)S(1)} %select_convert_fusion.3), channel_id=1, source_target_pairs={{0,4},{4,8},{8,12},{1,5},{5,9},{9,13},{2,6},{6,10},{10,14},{3,7},{... | collective-permute-start | bytes 98312 | tf_op jit(solution)/shard_map/while/body/eval_jaxpr/ppermute | solution.py:29
  128.2 3.2 %collective-permute-start.1 = (bf16[2,8,1024]{2,1,0:T(8,128)(2,1)S(1)}, bf16[2,8,1024]{2,1,0:T(8,128)(2,1)S(1)}, u32[]{:S(2)}, u32[]{:S(2)}) collective-permute-start(bf16[2,8,1024]{2,1,0:T(8,128)(2,1)S(1)} %collective-permute-done), channel_id=1, source_target_pairs={{2,0},{3,1},{6,4},{7,5},{10,8},{11,9},{14,12},{15,13},{18,16},{19,... | collective-permute-start | bytes 98312 | tf_op jit(solution)/shard_map/while/body/eval_jaxpr/ppermute | solution.py:19
  129.8 5.8 %collective-permute-start.2 = (bf16[2,8,1024]{2,1,0:T(8,128)(2,1)S(1)}, bf16[2,8,1024]{2,1,0:T(8,128)(2,1)S(1)}, u32[]{:S(2)}, u32[]{:S(2)}) collective-permute-start(bf16[2,8,1024]{2,1,0:T(8,128)(2,1)S(1)} %collective-permute-done), channel_id=1, source_target_pairs={{0,2},{1,3},{4,6},{5,7},{8,10},{9,11},{12,14},{13,15},{16,18},{17,... | collective-permute-start | bytes 98312 | tf_op jit(solution)/shard_map/while/body/eval_jaxpr/ppermute | solution.py:17
  140.2 5.8 %collective-permute-start = (bf16[2,8,1024]{2,1,0:T(8,128)(2,1)S(1)}, bf16[2,8,1024]{2,1,0:T(8,128)(2,1)S(1)}, u32[]{:S(2)}, u32[]{:S(2)}) collective-permute-start(bf16[2,8,1024]{2,1,0:T(8,128)(2,1)S(1)} %select_convert_fusion.3), channel_id=1, source_target_pairs={{0,4},{4,8},{8,12},{1,5},{5,9},{9,13},{2,6},{6,10},{10,14},{3,7},{... | collective-permute-start | bytes 98312 | tf_op jit(solution)/shard_map/while/body/eval_jaxpr/ppermute | solution.py:29
  146.0 3.2 %collective-permute-start.1 = (bf16[2,8,1024]{2,1,0:T(8,128)(2,1)S(1)}, bf16[2,8,1024]{2,1,0:T(8,128)(2,1)S(1)}, u32[]{:S(2)}, u32[]{:S(2)}) collective-permute-start(bf16[2,8,1024]{2,1,0:T(8,128)(2,1)S(1)} %collective-permute-done), channel_id=1, source_target_pairs={{2,0},{3,1},{6,4},{7,5},{10,8},{11,9},{14,12},{15,13},{18,16},{19,... | collective-permute-start | bytes 98312 | tf_op jit(solution)/shard_map/while/body/eval_jaxpr/ppermute | solution.py:19
  147.6 5.8 %collective-permute-start.2 = (bf16[2,8,1024]{2,1,0:T(8,128)(2,1)S(1)}, bf16[2,8,1024]{2,1,0:T(8,128)(2,1)S(1)}, u32[]{:S(2)}, u32[]{:S(2)}) collective-permute-start(bf16[2,8,1024]{2,1,0:T(8,128)(2,1)S(1)} %collective-permute-done), channel_id=1, source_target_pairs={{0,2},{1,3},{4,6},{5,7},{8,10},{9,11},{12,14},{13,15},{16,18},{17,... | collective-permute-start | bytes 98312 | tf_op jit(solution)/shard_map/while/body/eval_jaxpr/ppermute | solution.py:17
  157.9 5.8 %collective-permute-start = (bf16[2,8,1024]{2,1,0:T(8,128)(2,1)S(1)}, bf16[2,8,1024]{2,1,0:T(8,128)(2,1)S(1)}, u32[]{:S(2)}, u32[]{:S(2)}) collective-permute-start(bf16[2,8,1024]{2,1,0:T(8,128)(2,1)S(1)} %select_convert_fusion.3), channel_id=1, source_target_pairs={{0,4},{4,8},{8,12},{1,5},{5,9},{9,13},{2,6},{6,10},{10,14},{3,7},{... | collective-permute-start | bytes 98312 | tf_op jit(solution)/shard_map/while/body/eval_jaxpr/ppermute | solution.py:29
  163.7 3.2 %collective-permute-start.1 = (bf16[2,8,1024]{2,1,0:T(8,128)(2,1)S(1)}, bf16[2,8,1024]{2,1,0:T(8,128)(2,1)S(1)}, u32[]{:S(2)}, u32[]{:S(2)}) collective-permute-start(bf16[2,8,1024]{2,1,0:T(8,128)(2,1)S(1)} %collective-permute-done), channel_id=1, source_target_pairs={{2,0},{3,1},{6,4},{7,5},{10,8},{11,9},{14,12},{15,13},{18,16},{19,... | collective-permute-start | bytes 98312 | tf_op jit(solution)/shard_map/while/body/eval_jaxpr/ppermute | solution.py:19
  165.3 5.8 %collective-permute-start.2 = (bf16[2,8,1024]{2,1,0:T(8,128)(2,1)S(1)}, bf16[2,8,1024]{2,1,0:T(8,128)(2,1)S(1)}, u32[]{:S(2)}, u32[]{:S(2)}) collective-permute-start(bf16[2,8,1024]{2,1,0:T(8,128)(2,1)S(1)} %collective-permute-done), channel_id=1, source_target_pairs={{0,2},{1,3},{4,6},{5,7},{8,10},{9,11},{12,14},{13,15},{16,18},{17,... | collective-permute-start | bytes 98312 | tf_op jit(solution)/shard_map/while/body/eval_jaxpr/ppermute | solution.py:17
  (5 other events, 4.6 us)
Sparse Core Ops, SparseCore 0:
  75.5 19.0 all-reduce.8
where the time goes:
time: 183 us
  other arithmetic  66.1 us (36%)
  waiting for transfers between devices  51.1 us (28%)
  starting transfers between devices  39.3 us (21%)
  between operations  15.4 us (8%)
  local copies, waits for them, and re-layouts  5.6 us (3%)
  matrix products  4.26 us (2%)
    ppermute x7, waiting for transfers between devices, with_halo(): lax.ppermute(tail, axis, [(i, (i + 1) % count) for i in range(ends)])  29 us
    dot_general x9, other arithmetic, local(): jnp.einsum('cspw,cspw->spw', current, earlier[:, :, shift_y:shift_y + str...  24.6 us
    ppermute x5, starting transfers between devices, from_behind(): return lax.ppermute(value, axis, pairs)  17 us
    select_n x8, other arithmetic, compose(): updated = jnp.where(valid_rows, updated, 0.0)  15.3 us
    another operation x3, other arithmetic, local(): warped = jnp.stack(warped_list)  14 us
    ppermute x7, starting transfers between devices, with_halo(): lax.ppermute(head, axis, [((i + 1) % count, i) for i in range(ends)])  13.2 us
    ppermute x5, waiting for transfers between devices, from_behind(): return lax.ppermute(value, axis, pairs)  11.5 us
    ppermute x7, starting transfers between devices, with_halo(): lax.ppermute(tail, axis, [(i, (i + 1) % count) for i in range(ends)])  9.04 us
  transfers between devices with their start and end apart: 20, of which 19 were waited for; matrix products, arithmetic and copies ran while one was open for 10% of the time, Pallas kernels for 0%

commit v1 on v0

--- a/solution.py
+++ b/solution.py
@@ -4,6 +4,7 @@
 from jax.sharding import PartitionSpec as P
 
 score_scale = 4.0
+targets_save = lambda piece_in: jnp.sum(lax.all_gather(piece_in, "chan"), 0)
 
 
 def with_halo(cells, sides, width):
@@ -142,7 +143,7 @@
         along_x = along_x * rescale + jnp.sum(weights * step_cols, axis=0)
         running_max = highest
     head_flow = jnp.stack([along_y / weight_sum, along_x / weight_sum], axis=1)
-    flow_field = lax.psum(head_flow.astype(jnp.bfloat16), "chan").astype(jnp.float32) / chan_count
+    flow_field = targets_save(head_flow.astype(jnp.bfloat16)).astype(jnp.float32) / chan_count
     warped_list = []
     for local_sec in range(sec_local):
         source = jnp.pad(framed[:, local_sec + 1], ((0, 0), (0, 0), (4, 4)))

time: 183 us -> 163 us (0.89)
  between operations: 15.4 us -> 2.02 us
  waiting for transfers between devices: 51.1 us -> 42.1 us
  starting transfers between devices: 39.3 us -> 41.6 us
  blocking collectives: 0 us -> 1.9 us
    psum x1 -> x0, waiting for transfers between devices: 5.02 us -> none  [local(): lax.psum(head_flow.astype(jnp.bfloat16), 'chan').astype(jnp.float32)]
    ppermute x7, waiting for transfers between devices: 29 us -> 25.3 us  [with_halo(): lax.ppermute(tail, axis, [(i, (i + 1) % count) for i in range(ends)])]
    ppermute x7, starting transfers between devices: 13.2 us -> 15.2 us  [with_halo(): lax.ppermute(head, axis, [((i + 1) % count, i) for i in range(ends)])]
    all_gather x0 -> x1, blocking collectives: none -> 1.9 us  [targets_save = lambda piece_in: jnp.sum(lax.all_gather(piece_in, 'chan'), 0)]
  transfers between devices with their start and end apart: 20 -> 19, of which waited for: 19 -> 17; matrix products, arithmetic and copies ran while one was open for 10% -> 11% of each run, Pallas kernels for 0% -> 0%
where the time goes in v1:
time: 163 us; the launch traced here: 162 us
  other arithmetic  64.4 us (40%)
  waiting for transfers between devices  42.1 us (26%)
  starting transfers between devices  41.6 us (26%)
  local copies, waits for them, and re-layouts  5.6 us (3%)
  matrix products  4.26 us (3%)
  between operations  2.02 us (1%)
  blocking collectives  1.9 us (1%)
    ppermute x7, waiting for transfers between devices, with_halo(): lax.ppermute(tail, axis, [(i, (i + 1) % count) for i in range(ends)])  25.3 us
    dot_general x9, other arithmetic, local(): jnp.einsum('cspw,cspw->spw', current, earlier[:, :, shift_y:shift_y + str...  24.3 us
    ppermute x5, starting transfers between devices, from_behind(): return lax.ppermute(value, axis, pairs)  17.3 us
    select_n x8, other arithmetic, compose(): updated = jnp.where(valid_rows, updated, 0.0)  15.3 us
    ppermute x7, starting transfers between devices, with_halo(): lax.ppermute(head, axis, [((i + 1) % count, i) for i in range(ends)])  15.2 us
    another operation x3, other arithmetic, local(): warped = jnp.stack(warped_list)  14 us
    ppermute x5, waiting for transfers between devices, from_behind(): return lax.ppermute(value, axis, pairs)  11.2 us
    ppermute x7, starting transfers between devices, with_halo(): lax.ppermute(tail, axis, [(i, (i + 1) % count) for i in range(ends)])  9.04 us
  transfers between devices with their start and end apart: 19, of which 17 were waited for; matrix products, arithmetic and copies ran while one was open for 11% of the time, Pallas kernels for 0%

profile of v1, /device:TPU:10, one launch (start us, length us, event | category | flops | bytes accessed | tf_op | source)
XLA Modules:
  0.0 162.2 jit_solution(11245004049252585559)
XLA Ops:
  1.5 2.4 %collective-permute-start.4 = (bf16[2,3,1024]{2,1,0:T(4,128)(2,1)S(1)}, bf16[2,3,1024]{2,1,0:T(4,128)(2,1)S(1)}, u32[]{:S(2)}, u32[]{:S(2)}) collective-permute-start(bf16[2,3,1024]{2,1,0:T(4,128)(2,1)S(1)} %get-tuple-element.609), channel_id=1, source_target_pairs={{2,0},{3,1},{6,4},{7,5},{10,8},{11,9},{14,12},{15,13},{18,16},{19,... | collective-permute-start | bytes 36872 | tf_op jit(solution)/shard_map/ppermute | solution.py:20
  5.4 4.2 %collective-permute-done.3 = bf16[2,3,1024]{2,1,0:T(4,128)(2,1)S(1)} collective-permute-done((bf16[2,3,1024]{2,1,0:T(4,128)(2,1)S(1)}, bf16[2,3,1024]{2,1,0:T(4,128)(2,1)S(1)}, u32[]{:S(2)}, u32[]{:S(2)}) %collective-permute-start.3) | collective-permute-done | bytes 12320 | tf_op jit(solution)/shard_map/ppermute | solution.py:18
  12.1 2.0 %stack.348 = bf16[9,2,10,1024]{3,0,2,1:T(8,128)(2,1)S(1)} concatenate(bf16[1,2,10,1024]{3,0,2,1:T(2,128)(2,1)S(1)} %copy.252, bf16[1,2,10,1024]{3,0,2,1:T(2,128)(2,1)S(1)} %copy.253, bf16[1,2,10,1024]{3,0,2,1:T(2,128)(2,1)S(1)} %copy.254, bf16[1,2,10,1024]{3,0,2,1:T(2,128)(2,1)S(1)} %copy.255, bf16[1,2,10,1024]{3,0,2,1:T(2,128)(2,1)S(1)} %copy.256, ...), dimensions={0} | concatenate | bytes 737280 | tf_op jit(solution)/shard_map/stack | solution.py:46
  18.5 3.5 %collective-permute-start.5 = (bf16[16,1,8,1024]{3,0,2,1:T(8,128)(2,1)S(1)}, bf16[16,1,8,1024]{3,0,2,1:T(8,128)(2,1)S(1)}, u32[]{:S(2)}, u32[]{:S(2)}) collective-permute-start(bf16[16,1,8,1024]{3,0,2,1:T(8,128)(2,1)S(1)} %slice.2649), channel_id=1, source_target_pairs={{0,4},{4,8},{8,12},{1,5},{5,9},{9,13},{2,6},{6,10},{10,14},{3,7},{... | collective-permute-start | bytes 786440 | tf_op jit(solution)/shard_map/ppermute | solution.py:30
  22.9 4.1 %collective-permute-done.5 = bf16[16,1,8,1024]{3,0,2,1:T(8,128)(2,1)S(1)} collective-permute-done((bf16[16,1,8,1024]{3,0,2,1:T(8,128)(2,1)S(1)}, bf16[16,1,8,1024]{3,0,2,1:T(8,128)(2,1)S(1)}, u32[]{:S(2)}, u32[]{:S(2)}) %collective-permute-start.5) | collective-permute-done | bytes 262176 | tf_op jit(solution)/shard_map/ppermute | solution.py:30
  30.6 4.7 %collective-permute-done.7 = bf16[16,3,4,1024]{3,0,2,1:T(8,128)(2,1)S(1)} collective-permute-done((bf16[16,3,4,1024]{3,0,2,1:T(8,128)(2,1)S(1)}, bf16[16,3,4,1024]{3,0,2,1:T(8,128)(2,1)S(1)}, u32[]{:S(2)}, u32[]{:S(2)}) %collective-permute-start.7) | collective-permute-done | bytes 393248 | tf_op jit(solution)/shard_map/ppermute | solution.py:20
  35.3 4.1 %collective-permute-done.6 = bf16[16,3,4,1024]{3,0,2,1:T(8,128)(2,1)S(1)} collective-permute-done((bf16[16,3,4,1024]{3,0,2,1:T(8,128)(2,1)S(1)}, bf16[16,3,4,1024]{3,0,2,1:T(8,128)(2,1)S(1)}, u32[]{:S(2)}, u32[]{:S(2)}) %collective-permute-start.6) | collective-permute-done | bytes 393248 | tf_op jit(solution)/shard_map/ppermute | solution.py:18
  39.8 2.9 %fusion.345 = (f32[2,8,1024]{2,1,0:T(8,128)S(1)}, f32[2,8,1024]{2,1,0:T(8,128)S(1)}, f32[2,8,1024]{2,1,0:T(8,128)S(1)}, f32[2,8,1024]{2,1,0:T(8,128)S(1)}, f32[2...) fusion(bf16[16,2,8,1024]{3,0,2,1:T(8,128)(2,1)S(1)} %fusion.336, ...), kind=kLoop, calls=%fused_computation.661 | loop fusion | flops 7192576 | bytes 2162688 | tf_op jit(solution)/shard_map/cspw,cspw->spw/dot_general | solution.py:126
  42.8 2.8 %fusion.408 = (f32[2,8,1024]{2,1,0:T(8,128)S(1)}, f32[2,8,1024]{2,1,0:T(8,128)S(1)}, f32[2,8,1024]{2,1,0:T(8,128)S(1)}, f32[2,8,1024]{2,1,0:T(8,128)S(1)}, f32[2...) fusion(bf16[16,2,8,1024]{3,0,2,1:T(8,128)(2,1)S(1)} %fusion.336, ...), kind=kLoop, calls=%fused_computation.724 | loop fusion | flops 7192576 | bytes 2162688 | tf_op jit(solution)/shard_map/cspw,cspw->spw/dot_general | solution.py:126
  45.6 2.7 %fusion.397 = (f32[2,8,1024]{2,1,0:T(8,128)S(1)}, f32[2,8,1024]{2,1,0:T(8,128)S(1)}, f32[2,8,1024]{2,1,0:T(8,128)S(1)}, f32[2,8,1024]{2,1,0:T(8,128)S(1)}, f32[2...) fusion(bf16[16,2,8,1024]{3,0,2,1:T(8,128)(2,1)S(1)} %fusion.336, ...), kind=kLoop, calls=%fused_computation.713 | loop fusion | flops 7192576 | bytes 2162688 | tf_op jit(solution)/shard_map/cspw,cspw->spw/dot_general | solution.py:126
  48.3 2.7 %fusion.407 = (f32[2,8,1024]{2,1,0:T(8,128)S(1)}, f32[2,8,1024]{2,1,0:T(8,128)S(1)}, f32[2,8,1024]{2,1,0:T(8,128)S(1)}, f32[2,8,1024]{2,1,0:T(8,128)S(1)}, f32[2...) fusion(bf16[16,2,8,1024]{3,0,2,1:T(8,128)(2,1)S(1)} %fusion.336, ...), kind=kLoop, calls=%fused_computation.723 | loop fusion | flops 7192576 | bytes 2162688 | tf_op jit(solution)/shard_map/cspw,cspw->spw/dot_general | solution.py:126
  50.9 2.8 %fusion.376 = (f32[2,8,1024]{2,1,0:T(8,128)S(1)}, f32[2,8,1024]{2,1,0:T(8,128)S(1)}, f32[2,8,1024]{2,1,0:T(8,128)S(1)}, f32[2,8,1024]{2,1,0:T(8,128)S(1)}, f32[2...) fusion(bf16[16,2,8,1024]{3,0,2,1:T(8,128)(2,1)S(1)} %fusion.336, ...), kind=kLoop, calls=%fused_computation.692 | loop fusion | flops 7192576 | bytes 2162688 | tf_op jit(solution)/shard_map/cspw,cspw->spw/dot_general | solution.py:126
  53.7 2.8 %fusion.387 = (f32[2,8,1024]{2,1,0:T(8,128)S(1)}, f32[2,8,1024]{2,1,0:T(8,128)S(1)}, f32[2,8,1024]{2,1,0:T(8,128)S(1)}, f32[2,8,1024]{2,1,0:T(8,128)S(1)}, f32[2...) fusion(bf16[16,2,8,1024]{3,0,2,1:T(8,128)(2,1)S(1)} %fusion.336, ...), kind=kLoop, calls=%fused_computation.703 | loop fusion | flops 7192576 | bytes 2162688 | tf_op jit(solution)/shard_map/cspw,cspw->spw/dot_general | solution.py:126
  56.5 2.7 %fusion.356 = (f32[2,8,1024]{2,1,0:T(8,128)S(1)}, f32[2,8,1024]{2,1,0:T(8,128)S(1)}, f32[2,8,1024]{2,1,0:T(8,128)S(1)}, f32[2,8,1024]{2,1,0:T(8,128)S(1)}, f32[2...) fusion(bf16[16,2,8,1024]{3,0,2,1:T(8,128)(2,1)S(1)} %fusion.336, ...), kind=kLoop, calls=%fused_computation.672 | loop fusion | flops 7192576 | bytes 2162688 | tf_op jit(solution)/shard_map/cspw,cspw->spw/dot_general | solution.py:126
  59.2 2.9 %fusion.366 = (f32[2,8,1024]{2,1,0:T(8,128)S(1)}, f32[2,8,1024]{2,1,0:T(8,128)S(1)}, f32[2,8,1024]{2,1,0:T(8,128)S(1)}, f32[2,8,1024]{2,1,0:T(8,128)S(1)}, f32[2...) fusion(bf16[16,2,8,1024]{3,0,2,1:T(8,128)(2,1)S(1)} %fusion.336, ...), kind=kLoop, calls=%fused_computation.682 | loop fusion | flops 7192576 | bytes 2162688 | tf_op jit(solution)/shard_map/cspw,cspw->spw/dot_general | solution.py:126
  62.4 2.1 %fusion.404 = (f32[2,8,1024]{2,1,0:T(8,128)S(1)}, f32[2,8,1024]{2,1,0:T(8,128)S(1)}, f32[2,8,1024]{2,1,0:T(8,128)S(1)}, f32[2,8,1024]{2,1,0:T(8,128)S(1)}, f32[2...) fusion(bf16[16,3,12,1024]{3,0,2,1:T(8,128)(2,1)S(1)} %get-tuple, ...), kind=kLoop, calls=%fused_computation.720 | loop fusion | flops 7454720 | bytes 5570560 | tf_op jit(solution)/shard_map/cspw,cspw->spw/dot_general | solution.py:126
  72.8 7.0 %fusion.447 = bf16[1,16,8,1024]{3,1,2,0:T(8,128)(2,1)S(1)} fusion(f32[8,1024]{1,0:T(8,128)S(1)} %copy-done.10, f32[8,1024]{1,0:T(8,128)S(1)} %get-tuple-element.570, f32[8,1024]{1,0:T(8,128)S(1)} %get-tuple-element.569, f32[8,1024]{1,0:T(8,128)S(1)} %get-tuple-element.568, bf16[16,16,1024]{2,0,1:T(8,128)(2,1)S(1)} %get-tuple-element.543, ...), kind=kLoop, calls=%fused_computation.825 | loop fusion | flops 33030144 | bytes 3735552 | tf_op jit(solution)/shard_map/stack | solution.py:151
  79.8 7.0 %fusion.446 = bf16[1,16,8,1024]{3,1,2,0:T(8,128)(2,1)S(1)} fusion(f32[8,1024]{1,0:T(8,128)S(1)} %copy-done.8, f32[8,1024]{1,0:T(8,128)S(1)} %copy-done.7, f32[8,1024]{1,0:T(8,128)S(1)} %copy-done.6, f32[8,1024]{1,0:T(8,128)S(1)} %copy-done.5, bf16[16,16,1024]{2,0,1:T(8,128)(2,1)S(1)} %get-tuple-element.542, f32[8,1024]{1,0:T(8,128)S(1)} %copy-done.4, ...), kind=kLoop, calls=%fused_computation.824 | loop fusion | flops 33030144 | bytes 3735552 | tf_op jit(solution)/shard_map/stack | solution.py:151
  88.2 74.0 %while.16 = (s32[]{:T(128)}, f32[2,8,1024]{2,1,0:T(8,128)S(1)}, f32[2,2,8,1024]{3,2,1,0:T(8,128)}, s32[16,1]{0,1:T(1,128)S(1)}, f32[2,4,16,1024]{3,2,1,0:T(8,128...) while((s32[]{:T(128)}, f32[2,8,1024]{2,1,0:T(8,128)S(1)}, ...), condition=%wide.region_29.30_spmd.clone, body=%wide.region_28.29_spmd.clone.sunk | while | flops 12337227 | bytes 8586647 | solution.py:197
  88.2 3.5 %collective-permute-start = (bf16[2,8,1024]{2,1,0:T(8,128)(2,1)S(1)}, bf16[2,8,1024]{2,1,0:T(8,128)(2,1)S(1)}, u32[]{:S(2)}, u32[]{:S(2)}) collective-permute-start(bf16[2,8,1024]{2,1,0:T(8,128)(2,1)S(1)} %select_convert_fusion.3), channel_id=1, source_target_pairs={{0,4},{4,8},{8,12},{1,5},{5,9},{9,13},{2,6},{6,10},{10,14},{3,7},{... | collective-permute-start | bytes 98312 | tf_op jit(solution)/shard_map/while/body/eval_jaxpr/ppermute | solution.py:30
  94.0 4.5 %collective-permute-start.1 = (bf16[2,8,1024]{2,1,0:T(8,128)(2,1)S(1)}, bf16[2,8,1024]{2,1,0:T(8,128)(2,1)S(1)}, u32[]{:S(2)}, u32[]{:S(2)}) collective-permute-start(bf16[2,8,1024]{2,1,0:T(8,128)(2,1)S(1)} %collective-permute-done), channel_id=1, source_target_pairs={{2,0},{3,1},{6,4},{7,5},{10,8},{11,9},{14,12},{15,13},{18,16},{19,... | collective-permute-start | bytes 98312 | tf_op jit(solution)/shard_map/while/body/eval_jaxpr/ppermute | solution.py:20
  100.2 4.2 %collective-permute-done.2 = bf16[2,8,1024]{2,1,0:T(8,128)(2,1)S(1)} collective-permute-done((bf16[2,8,1024]{2,1,0:T(8,128)(2,1)S(1)}, bf16[2,8,1024]{2,1,0:T(8,128)(2,1)S(1)}, u32[]{:S(2)}, u32[]{:S(2)}) %collective-permute-start.2) | collective-permute-done | bytes 32800 | tf_op jit(solution)/shard_map/while/body/eval_jaxpr/ppermute | solution.py:18
  104.4 2.5 %fusion.538 = f32[2,16,1024]{2,1,0:T(8,128)S(1)} fusion(f32[2,24,1024]{2,1,0:T(8,128)S(1)} %maximum_convert_fusion.3, f32[2,4,16,1024]{3,2,1,0:T(8,128)S(1)} %get-tuple-element.825, f32[16,1024]{1,0:T(8,128)S(1)} %get-tuple-element.749, f32[16,1024]{1,0:T(8,128)S(1)} %get-tuple-element.750, f32[16,1024]{1,0:T(8,128)S(1)} %get-tuple-element.751, ...), kind=kLoop, calls=%fused_computation.244.clone.1 | loop fusion | flops 5701632 | bytes 2949632 | tf_op jit(solution)/shard_map/while/body/eval_jaxpr/jit(_where)/select_n | solution.py:183
  108.9 3.5 %collective-permute-start = (bf16[2,8,1024]{2,1,0:T(8,128)(2,1)S(1)}, bf16[2,8,1024]{2,1,0:T(8,128)(2,1)S(1)}, u32[]{:S(2)}, u32[]{:S(2)}) collective-permute-start(bf16[2,8,1024]{2,1,0:T(8,128)(2,1)S(1)} %select_convert_fusion.3), channel_id=1, source_target_pairs={{0,4},{4,8},{8,12},{1,5},{5,9},{9,13},{2,6},{6,10},{10,14},{3,7},{... | collective-permute-start | bytes 98312 | tf_op jit(solution)/shard_map/while/body/eval_jaxpr/ppermute | solution.py:30
  117.9 4.2 %collective-permute-done.2 = bf16[2,8,1024]{2,1,0:T(8,128)(2,1)S(1)} collective-permute-done((bf16[2,8,1024]{2,1,0:T(8,128)(2,1)S(1)}, bf16[2,8,1024]{2,1,0:T(8,128)(2,1)S(1)}, u32[]{:S(2)}, u32[]{:S(2)}) %collective-permute-start.2) | collective-permute-done | bytes 32800 | tf_op jit(solution)/shard_map/while/body/eval_jaxpr/ppermute | solution.py:18
  122.2 2.5 %fusion.538 = f32[2,16,1024]{2,1,0:T(8,128)S(1)} fusion(f32[2,24,1024]{2,1,0:T(8,128)S(1)} %maximum_convert_fusion.3, f32[2,4,16,1024]{3,2,1,0:T(8,128)S(1)} %get-tuple-element.825, f32[16,1024]{1,0:T(8,128)S(1)} %get-tuple-element.749, f32[16,1024]{1,0:T(8,128)S(1)} %get-tuple-element.750, f32[16,1024]{1,0:T(8,128)S(1)} %get-tuple-element.751, ...), kind=kLoop, calls=%fused_computation.244.clone.1 | loop fusion | flops 5701632 | bytes 2949632 | tf_op jit(solution)/shard_map/while/body/eval_jaxpr/jit(_where)/select_n | solution.py:183
  126.7 3.5 %collective-permute-start = (bf16[2,8,1024]{2,1,0:T(8,128)(2,1)S(1)}, bf16[2,8,1024]{2,1,0:T(8,128)(2,1)S(1)}, u32[]{:S(2)}, u32[]{:S(2)}) collective-permute-start(bf16[2,8,1024]{2,1,0:T(8,128)(2,1)S(1)} %select_convert_fusion.3), channel_id=1, source_target_pairs={{0,4},{4,8},{8,12},{1,5},{5,9},{9,13},{2,6},{6,10},{10,14},{3,7},{... | collective-permute-start | bytes 98312 | tf_op jit(solution)/shard_map/while/body/eval_jaxpr/ppermute | solution.py:30
  135.7 4.2 %collective-permute-done.2 = bf16[2,8,1024]{2,1,0:T(8,128)(2,1)S(1)} collective-permute-done((bf16[2,8,1024]{2,1,0:T(8,128)(2,1)S(1)}, bf16[2,8,1024]{2,1,0:T(8,128)(2,1)S(1)}, u32[]{:S(2)}, u32[]{:S(2)}) %collective-permute-start.2) | collective-permute-done | bytes 32800 | tf_op jit(solution)/shard_map/while/body/eval_jaxpr/ppermute | solution.py:18
  139.9 2.5 %fusion.538 = f32[2,16,1024]{2,1,0:T(8,128)S(1)} fusion(f32[2,24,1024]{2,1,0:T(8,128)S(1)} %maximum_convert_fusion.3, f32[2,4,16,1024]{3,2,1,0:T(8,128)S(1)} %get-tuple-element.825, f32[16,1024]{1,0:T(8,128)S(1)} %get-tuple-element.749, f32[16,1024]{1,0:T(8,128)S(1)} %get-tuple-element.750, f32[16,1024]{1,0:T(8,128)S(1)} %get-tuple-element.751, ...), kind=kLoop, calls=%fused_computation.244.clone.1 | loop fusion | flops 5701632 | bytes 2949632 | tf_op jit(solution)/shard_map/while/body/eval_jaxpr/jit(_where)/select_n | solution.py:183
  144.4 3.5 %collective-permute-start = (bf16[2,8,1024]{2,1,0:T(8,128)(2,1)S(1)}, bf16[2,8,1024]{2,1,0:T(8,128)(2,1)S(1)}, u32[]{:S(2)}, u32[]{:S(2)}) collective-permute-start(bf16[2,8,1024]{2,1,0:T(8,128)(2,1)S(1)} %select_convert_fusion.3), channel_id=1, source_target_pairs={{0,4},{4,8},{8,12},{1,5},{5,9},{9,13},{2,6},{6,10},{10,14},{3,7},{... | collective-permute-start | bytes 98312 | tf_op jit(solution)/shard_map/while/body/eval_jaxpr/ppermute | solution.py:30
  153.4 4.2 %collective-permute-done.2 = bf16[2,8,1024]{2,1,0:T(8,128)(2,1)S(1)} collective-permute-done((bf16[2,8,1024]{2,1,0:T(8,128)(2,1)S(1)}, bf16[2,8,1024]{2,1,0:T(8,128)(2,1)S(1)}, u32[]{:S(2)}, u32[]{:S(2)}) %collective-permute-start.2) | collective-permute-done | bytes 32800 | tf_op jit(solution)/shard_map/while/body/eval_jaxpr/ppermute | solution.py:18
  157.7 2.5 %fusion.538 = f32[2,16,1024]{2,1,0:T(8,128)S(1)} fusion(f32[2,24,1024]{2,1,0:T(8,128)S(1)} %maximum_convert_fusion.3, f32[2,4,16,1024]{3,2,1,0:T(8,128)S(1)} %get-tuple-element.825, f32[16,1024]{1,0:T(8,128)S(1)} %get-tuple-element.749, f32[16,1024]{1,0:T(8,128)S(1)} %get-tuple-element.750, f32[16,1024]{1,0:T(8,128)S(1)} %get-tuple-element.751, ...), kind=kLoop, calls=%fused_computation.244.clone.1 | loop fusion | flops 5701632 | bytes 2949632 | tf_op jit(solution)/shard_map/while/body/eval_jaxpr/jit(_where)/select_n | solution.py:183
  (249 shorter events, 51.0 us)
Async XLA Ops:
  0.6 14.1 %copy-start = (bf16[9,32,32]{2,1,0:T(8,128)(2,1)S(1)}, bf16[9,32,32]{2,1,0:T(8,128)(2,1)}, u32[]{:S(2)}) copy-start(bf16[9,32,32]{2,1,0:T(8,128)(2,1)} %param.8) | copy-start | bytes 55300
  1.5 3.9 %collective-permute-start.4 = (bf16[2,3,1024]{2,1,0:T(4,128)(2,1)S(1)}, bf16[2,3,1024]{2,1,0:T(4,128)(2,1)S(1)}, u32[]{:S(2)}, u32[]{:S(2)}) collective-permute-start(bf16[2,3,1024]{2,1,0:T(4,128)(2,1)S(1)} %get-tuple-element.609), channel_id=1, source_target_pairs={{2,0},{3,1},{6,4},{7,5},{10,8},{11,9},{14,12},{15,13},{18,16},{19,... | collective-permute-start | bytes 36872 | tf_op jit(solution)/shard_map/ppermute | solution.py:20
  3.9 5.6 %collective-permute-start.3 = (bf16[2,3,1024]{2,1,0:T(4,128)(2,1)S(1)}, bf16[2,3,1024]{2,1,0:T(4,128)(2,1)S(1)}, u32[]{:S(2)}, u32[]{:S(2)}) collective-permute-start(bf16[2,3,1024]{2,1,0:T(4,128)(2,1)S(1)} %get-tuple-element.608), channel_id=1, source_target_pairs={{0,2},{1,3},{4,6},{5,7},{8,10},{9,11},{12,14},{13,15},{16,18},{17,... | collective-permute-start | bytes 36872 | tf_op jit(solution)/shard_map/ppermute | solution.py:18
  18.5 8.5 %collective-permute-start.5 = (bf16[16,1,8,1024]{3,0,2,1:T(8,128)(2,1)S(1)}, bf16[16,1,8,1024]{3,0,2,1:T(8,128)(2,1)S(1)}, u32[]{:S(2)}, u32[]{:S(2)}) collective-permute-start(bf16[16,1,8,1024]{3,0,2,1:T(8,128)(2,1)S(1)} %slice.2649), channel_id=1, source_target_pairs={{0,4},{4,8},{8,12},{1,5},{5,9},{9,13},{2,6},{6,10},{10,14},{3,7},{... | collective-permute-start | bytes 786440 | tf_op jit(solution)/shard_map/ppermute | solution.py:30
  27.1 8.2 %collective-permute-start.7 = (bf16[16,3,4,1024]{3,0,2,1:T(8,128)(2,1)S(1)}, bf16[16,3,4,1024]{3,0,2,1:T(8,128)(2,1)S(1)}, u32[]{:S(2)}, u32[]{:S(2)}) collective-permute-start(bf16[16,3,4,1024]{3,0,2,1:T(8,128)(2,1)S(1)} %get-tuple-element.547), channel_id=1, source_target_pairs={{2,0},{3,1},{6,4},{7,5},{10,8},{11,9},{14,12},{15,13},{18,16},{19,... | collective-permute-start | bytes 1179656 | tf_op jit(solution)/shard_map/ppermute | solution.py:20
  29.0 10.4 %collective-permute-start.6 = (bf16[16,3,4,1024]{3,0,2,1:T(8,128)(2,1)S(1)}, bf16[16,3,4,1024]{3,0,2,1:T(8,128)(2,1)S(1)}, u32[]{:S(2)}, u32[]{:S(2)}) collective-permute-start(bf16[16,3,4,1024]{3,0,2,1:T(8,128)(2,1)S(1)} %get-tuple-element.546), channel_id=1, source_target_pairs={{0,2},{1,3},{4,6},{5,7},{8,10},{9,11},{12,14},{13,15},{16,18},{17,... | collective-permute-start | bytes 1179656 | tf_op jit(solution)/shard_map/ppermute | solution.py:18
  67.6 5.1 %copy-start.10 = (f32[8,1024]{1,0:T(8,128)S(1)}, f32[8,1024]{1,0:T(8,128)}, u32[]{:S(2)}) copy-start(f32[8,1024]{1,0:T(8,128)} %get-tuple-element.588) | copy-start | bytes 98308
  67.6 5.1 %copy-start.11 = (f32[8,1024]{1,0:T(8,128)S(1)}, f32[8,1024]{1,0:T(8,128)}, u32[]{:S(2)}) copy-start(f32[8,1024]{1,0:T(8,128)} %get-tuple-element.589) | copy-start | bytes 98308
  67.6 5.1 %copy-start.12 = (f32[8,1024]{1,0:T(8,128)S(1)}, f32[8,1024]{1,0:T(8,128)}, u32[]{:S(2)}) copy-start(f32[8,1024]{1,0:T(8,128)} %get-tuple-element.590) | copy-start | bytes 98308
  67.6 5.1 %copy-start.13 = (f32[8,1024]{1,0:T(8,128)S(1)}, f32[8,1024]{1,0:T(8,128)}, u32[]{:S(2)}) copy-start(f32[8,1024]{1,0:T(8,128)} %get-tuple-element.591) | copy-start | bytes 98308
  69.9 18.1 %collective-permute-start.9 = (bf16[2,4,4,1024]{3,2,1,0:T(4,128)(2,1)S(1)}, bf16[2,4,4,1024]{3,2,1,0:T(4,128)(2,1)S(1)}, u32[]{:S(2)}, u32[]{:S(2)}) collective-permute-start(bf16[2,4,4,1024]{3,2,1,0:T(4,128)(2,1)S(1)} %get-tuple-element.557), channel_id=1, source_target_pairs={{2,0},{3,1},{6,4},{7,5},{10,8},{11,9},{14,12},{15,13},{18,16},{19,... | collective-permute-start | bytes 196616 | tf_op jit(solution)/shard_map/ppermute | solution.py:20
  71.3 16.6 %collective-permute-start.8 = (bf16[2,4,4,1024]{3,2,1,0:T(4,128)(2,1)S(1)}, bf16[2,4,4,1024]{3,2,1,0:T(4,128)(2,1)S(1)}, u32[]{:S(2)}, u32[]{:S(2)}) collective-permute-start(bf16[2,4,4,1024]{3,2,1,0:T(4,128)(2,1)S(1)} %get-tuple-element.556), channel_id=1, source_target_pairs={{0,2},{1,3},{4,6},{5,7},{8,10},{9,11},{12,14},{13,15},{16,18},{17,... | collective-permute-start | bytes 196616 | tf_op jit(solution)/shard_map/ppermute | solution.py:18
  72.7 7.1 %copy-start.2 = (f32[8,1024]{1,0:T(8,128)S(1)}, f32[8,1024]{1,0:T(8,128)}, u32[]{:S(2)}) copy-start(f32[8,1024]{1,0:T(8,128)} %get-tuple-element.580) | copy-start | bytes 98308
  72.7 7.1 %copy-start.3 = (f32[8,1024]{1,0:T(8,128)S(1)}, f32[8,1024]{1,0:T(8,128)}, u32[]{:S(2)}) copy-start(f32[8,1024]{1,0:T(8,128)} %get-tuple-element.581) | copy-start | bytes 98308
  72.7 7.1 %copy-start.4 = (f32[8,1024]{1,0:T(8,128)S(1)}, f32[8,1024]{1,0:T(8,128)}, u32[]{:S(2)}) copy-start(f32[8,1024]{1,0:T(8,128)} %get-tuple-element.582) | copy-start | bytes 98308
  72.7 7.1 %copy-start.5 = (f32[8,1024]{1,0:T(8,128)S(1)}, f32[8,1024]{1,0:T(8,128)}, u32[]{:S(2)}) copy-start(f32[8,1024]{1,0:T(8,128)} %get-tuple-element.583) | copy-start | bytes 98308
  72.7 7.1 %copy-start.6 = (f32[8,1024]{1,0:T(8,128)S(1)}, f32[8,1024]{1,0:T(8,128)}, u32[]{:S(2)}) copy-start(f32[8,1024]{1,0:T(8,128)} %get-tuple-element.584) | copy-start | bytes 98308
  72.7 7.1 %copy-start.7 = (f32[8,1024]{1,0:T(8,128)S(1)}, f32[8,1024]{1,0:T(8,128)}, u32[]{:S(2)}) copy-start(f32[8,1024]{1,0:T(8,128)} %get-tuple-element.585) | copy-start | bytes 98308
  72.8 7.1 %copy-start.8 = (f32[8,1024]{1,0:T(8,128)S(1)}, f32[8,1024]{1,0:T(8,128)}, u32[]{:S(2)}) copy-start(f32[8,1024]{1,0:T(8,128)} %get-tuple-element.586) | copy-start | bytes 98308
  72.8 7.1 %copy-start.9 = (f32[8,1024]{1,0:T(8,128)S(1)}, f32[8,1024]{1,0:T(8,128)}, u32[]{:S(2)}) copy-start(f32[8,1024]{1,0:T(8,128)} %get-tuple-element.587) | copy-start | bytes 98308
  88.2 5.8 %collective-permute-start = (bf16[2,8,1024]{2,1,0:T(8,128)(2,1)S(1)}, bf16[2,8,1024]{2,1,0:T(8,128)(2,1)S(1)}, u32[]{:S(2)}, u32[]{:S(2)}) collective-permute-start(bf16[2,8,1024]{2,1,0:T(8,128)(2,1)S(1)} %select_convert_fusion.3), channel_id=1, source_target_pairs={{0,4},{4,8},{8,12},{1,5},{5,9},{9,13},{2,6},{6,10},{10,14},{3,7},{... | collective-permute-start | bytes 98312 | tf_op jit(solution)/shard_map/while/body/eval_jaxpr/ppermute | solution.py:30
  94.0 6.1 %collective-permute-start.1 = (bf16[2,8,1024]{2,1,0:T(8,128)(2,1)S(1)}, bf16[2,8,1024]{2,1,0:T(8,128)(2,1)S(1)}, u32[]{:S(2)}, u32[]{:S(2)}) collective-permute-start(bf16[2,8,1024]{2,1,0:T(8,128)(2,1)S(1)} %collective-permute-done), channel_id=1, source_target_pairs={{2,0},{3,1},{6,4},{7,5},{10,8},{11,9},{14,12},{15,13},{18,16},{19,... | collective-permute-start | bytes 98312 | tf_op jit(solution)/shard_map/while/body/eval_jaxpr/ppermute | solution.py:20
  98.6 5.8 %collective-permute-start.2 = (bf16[2,8,1024]{2,1,0:T(8,128)(2,1)S(1)}, bf16[2,8,1024]{2,1,0:T(8,128)(2,1)S(1)}, u32[]{:S(2)}, u32[]{:S(2)}) collective-permute-start(bf16[2,8,1024]{2,1,0:T(8,128)(2,1)S(1)} %collective-permute-done), channel_id=1, source_target_pairs={{0,2},{1,3},{4,6},{5,7},{8,10},{9,11},{12,14},{13,15},{16,18},{17,... | collective-permute-start | bytes 98312 | tf_op jit(solution)/shard_map/while/body/eval_jaxpr/ppermute | solution.py:18
  108.9 5.8 %collective-permute-start = (bf16[2,8,1024]{2,1,0:T(8,128)(2,1)S(1)}, bf16[2,8,1024]{2,1,0:T(8,128)(2,1)S(1)}, u32[]{:S(2)}, u32[]{:S(2)}) collective-permute-start(bf16[2,8,1024]{2,1,0:T(8,128)(2,1)S(1)} %select_convert_fusion.3), channel_id=1, source_target_pairs={{0,4},{4,8},{8,12},{1,5},{5,9},{9,13},{2,6},{6,10},{10,14},{3,7},{... | collective-permute-start | bytes 98312 | tf_op jit(solution)/shard_map/while/body/eval_jaxpr/ppermute | solution.py:30
  114.7 3.2 %collective-permute-start.1 = (bf16[2,8,1024]{2,1,0:T(8,128)(2,1)S(1)}, bf16[2,8,1024]{2,1,0:T(8,128)(2,1)S(1)}, u32[]{:S(2)}, u32[]{:S(2)}) collective-permute-start(bf16[2,8,1024]{2,1,0:T(8,128)(2,1)S(1)} %collective-permute-done), channel_id=1, source_target_pairs={{2,0},{3,1},{6,4},{7,5},{10,8},{11,9},{14,12},{15,13},{18,16},{19,... | collective-permute-start | bytes 98312 | tf_op jit(solution)/shard_map/while/body/eval_jaxpr/ppermute | solution.py:20
  116.3 5.8 %collective-permute-start.2 = (bf16[2,8,1024]{2,1,0:T(8,128)(2,1)S(1)}, bf16[2,8,1024]{2,1,0:T(8,128)(2,1)S(1)}, u32[]{:S(2)}, u32[]{:S(2)}) collective-permute-start(bf16[2,8,1024]{2,1,0:T(8,128)(2,1)S(1)} %collective-permute-done), channel_id=1, source_target_pairs={{0,2},{1,3},{4,6},{5,7},{8,10},{9,11},{12,14},{13,15},{16,18},{17,... | collective-permute-start | bytes 98312 | tf_op jit(solution)/shard_map/while/body/eval_jaxpr/ppermute | solution.py:18
  126.7 5.8 %collective-permute-start = (bf16[2,8,1024]{2,1,0:T(8,128)(2,1)S(1)}, bf16[2,8,1024]{2,1,0:T(8,128)(2,1)S(1)}, u32[]{:S(2)}, u32[]{:S(2)}) collective-permute-start(bf16[2,8,1024]{2,1,0:T(8,128)(2,1)S(1)} %select_convert_fusion.3), channel_id=1, source_target_pairs={{0,4},{4,8},{8,12},{1,5},{5,9},{9,13},{2,6},{6,10},{10,14},{3,7},{... | collective-permute-start | bytes 98312 | tf_op jit(solution)/shard_map/while/body/eval_jaxpr/ppermute | solution.py:30
  132.5 3.2 %collective-permute-start.1 = (bf16[2,8,1024]{2,1,0:T(8,128)(2,1)S(1)}, bf16[2,8,1024]{2,1,0:T(8,128)(2,1)S(1)}, u32[]{:S(2)}, u32[]{:S(2)}) collective-permute-start(bf16[2,8,1024]{2,1,0:T(8,128)(2,1)S(1)} %collective-permute-done), channel_id=1, source_target_pairs={{2,0},{3,1},{6,4},{7,5},{10,8},{11,9},{14,12},{15,13},{18,16},{19,... | collective-permute-start | bytes 98312 | tf_op jit(solution)/shard_map/while/body/eval_jaxpr/ppermute | solution.py:20
  134.1 5.8 %collective-permute-start.2 = (bf16[2,8,1024]{2,1,0:T(8,128)(2,1)S(1)}, bf16[2,8,1024]{2,1,0:T(8,128)(2,1)S(1)}, u32[]{:S(2)}, u32[]{:S(2)}) collective-permute-start(bf16[2,8,1024]{2,1,0:T(8,128)(2,1)S(1)} %collective-permute-done), channel_id=1, source_target_pairs={{0,2},{1,3},{4,6},{5,7},{8,10},{9,11},{12,14},{13,15},{16,18},{17,... | collective-permute-start | bytes 98312 | tf_op jit(solution)/shard_map/while/body/eval_jaxpr/ppermute | solution.py:18
  144.4 5.8 %collective-permute-start = (bf16[2,8,1024]{2,1,0:T(8,128)(2,1)S(1)}, bf16[2,8,1024]{2,1,0:T(8,128)(2,1)S(1)}, u32[]{:S(2)}, u32[]{:S(2)}) collective-permute-start(bf16[2,8,1024]{2,1,0:T(8,128)(2,1)S(1)} %select_convert_fusion.3), channel_id=1, source_target_pairs={{0,4},{4,8},{8,12},{1,5},{5,9},{9,13},{2,6},{6,10},{10,14},{3,7},{... | collective-permute-start | bytes 98312 | tf_op jit(solution)/shard_map/while/body/eval_jaxpr/ppermute | solution.py:30
  150.2 3.2 %collective-permute-start.1 = (bf16[2,8,1024]{2,1,0:T(8,128)(2,1)S(1)}, bf16[2,8,1024]{2,1,0:T(8,128)(2,1)S(1)}, u32[]{:S(2)}, u32[]{:S(2)}) collective-permute-start(bf16[2,8,1024]{2,1,0:T(8,128)(2,1)S(1)} %collective-permute-done), channel_id=1, source_target_pairs={{2,0},{3,1},{6,4},{7,5},{10,8},{11,9},{14,12},{15,13},{18,16},{19,... | collective-permute-start | bytes 98312 | tf_op jit(solution)/shard_map/while/body/eval_jaxpr/ppermute | solution.py:20
  151.9 5.8 %collective-permute-start.2 = (bf16[2,8,1024]{2,1,0:T(8,128)(2,1)S(1)}, bf16[2,8,1024]{2,1,0:T(8,128)(2,1)S(1)}, u32[]{:S(2)}, u32[]{:S(2)}) collective-permute-start(bf16[2,8,1024]{2,1,0:T(8,128)(2,1)S(1)} %collective-permute-done), channel_id=1, source_target_pairs={{0,2},{1,3},{4,6},{5,7},{8,10},{9,11},{12,14},{13,15},{16,18},{17,... | collective-permute-start | bytes 98312 | tf_op jit(solution)/shard_map/while/body/eval_jaxpr/ppermute | solution.py:18
  (4 other events, 16.6 us)
